TPU v7x, 128 devices: a whole 4x4x4 slice. The times are simulated.
128 devices in a mesh: req: 8 (over y, core), hid: 16 (over x, z).
Axes of the slice: x: 4, y: 4, z: 4, core: 2. Of those that a mesh axis runs over, the one named last changes fastest.
Arguments:
- tokens: bfloat16 [24576, 1536], P(('req', 'hid')), may hold values from -6 to 6
- segment: int32 [24576], P(('req', 'hid')), may hold values from 0 to 35, as said below
- attn_gain: float32 [1536], replicated, may hold values from 0.1 to 1.9
- w_query: bfloat16 [1536, 1536], replicated, may hold values from -0.2 to 0.2
- w_key: bfloat16 [1536, 512], replicated, may hold values from -0.2 to 0.2
- w_value: bfloat16 [1536, 512], replicated, may hold values from -0.15625 to 0.15625
- q_gain: float32 [64], replicated, may hold values from 0.5 to 6
- k_gain: float32 [64], replicated, may hold values from 0.5 to 6
- w_out: bfloat16 [1536, 1536], replicated, may hold values from -0.15625 to 0.15625
- ffn_gain: float32 [1536], replicated, may hold values from 0.1 to 1.9
- w_gate: bfloat16 [4608, 1536], P(('req', 'hid')), may hold values from -0.15625 to 0.15625
- w_up: bfloat16 [4608, 1536], P(('req', 'hid')), may hold values from -0.15625 to 0.15625
- w_down: bfloat16 [4608, 1536], P(('req', 'hid')), may hold values from -0.09375 to 0.09375
Outputs:
- mixed: bfloat16 [24576, 1536], P(('req', 'hid'))
- kv_cache: bfloat16 [24576, 1024], P(('req', 'hid'))
Inputs may be any that keep to these rules, and one draw needn't show every extreme that they name: Segment ids never fall along the tokens and start at 0. A segment never crosses a boundary between aligned blocks of 3072 tokens; the first block is one segment of exactly 3072 tokens, and every later block holds exactly five segments.
All inputs are finite; a program needn't handle non-finite values.
Results may differ from a plain program's by a relative error of at most 0.015.
Values may be sent and summed in bfloat16 or wider, within the bound.
No kernel may reach another device: no remote copies, remote signals or barrier semaphores. Data moves between devices by JAX's collectives and lax.ppermute only.
A program may use at most 128 MiB of HBM per device.

v0:
```python
import jax
import jax.numpy as jnp
from jax import lax
from jax.sharding import PartitionSpec as P

H = 24
KVH = 8
HD = 64
EPSILON = 1e-05
ROPE_BASE = 1000000.0
NEG_FILL = -1e30
SCORE_SCALE = 0.125


def rms_scale(values, gain):
    mean_sq = jnp.mean(values * values, axis=-1, keepdims=True)
    return values * lax.rsqrt(mean_sq + EPSILON) * gain


def seg_positions(seg_ids):
    indices = jnp.arange(seg_ids.shape[0], dtype=jnp.int32)
    is_first = jnp.concatenate([jnp.ones((1,), bool), seg_ids[1:] != seg_ids[:-1]])
    seg_begin = lax.cummax(jnp.where(is_first, indices, jnp.zeros_like(indices)), axis=0)
    return indices - seg_begin


def rotate(heads, positions):
    half_dim = heads.shape[-1] // 2
    inv_freq = ROPE_BASE ** (-(jnp.arange(half_dim, dtype=jnp.float32) * 2.0) / (2.0 * half_dim))
    angles = positions.astype(jnp.float32)[:, None] * inv_freq[None, :]
    cos_val = jnp.cos(angles)[:, None, :]
    sin_val = jnp.sin(angles)[:, None, :]
    left = heads[..., :half_dim]
    right = heads[..., half_dim:]
    return jnp.concatenate(
        [left * cos_val - right * sin_val, right * cos_val + left * sin_val], axis=-1
    )


def block_length(shard_rows):
    return 4 * shard_rows


def key_block(running, key_blk, val_blk, key_idx, q_grid, seg_start, query_idx):
    run_peak, run_total, run_acc = running
    k_grid = key_blk.reshape(-1, KVH, HD).transpose(1, 0, 2)
    v_grid = val_blk.reshape(-1, KVH, HD).transpose(1, 0, 2)
    scores = (
        jnp.einsum("kgqd,kcd->kgqc", q_grid, k_grid, preferred_element_type=jnp.float32)
        * SCORE_SCALE
    )
    allowed = (key_idx[None, :] <= query_idx[:, None]) & (key_idx[None, :] >= seg_start[:, None])
    scores = jnp.where(allowed, scores, NEG_FILL)
    new_peak = jnp.maximum(run_peak, jnp.max(scores, axis=-1))
    weights = jnp.where(allowed, jnp.exp(scores - new_peak[..., None]), 0.0)
    factor = jnp.exp(run_peak - new_peak)
    new_total = run_total * factor + jnp.sum(weights, axis=-1)
    product = jnp.einsum(
        "kgqc,kcd->kgqd", weights.astype(jnp.bfloat16), v_grid, preferred_element_type=jnp.float32
    )
    return (new_peak, new_total, run_acc * factor[..., None] + product)


def unit_terms(pieces, gathered):
    gate_part, up_part, down_part = pieces
    contract = (((1,), (1,)), ((), ()))
    gate_act = lax.dot_general(gathered, gate_part, contract, preferred_element_type=jnp.float32)
    up_act = lax.dot_general(gathered, up_part, contract, preferred_element_type=jnp.float32)
    hidden = (jax.nn.silu(gate_act) * up_act).astype(jnp.bfloat16)
    return jnp.dot(hidden, down_part, preferred_element_type=jnp.float32)


def gather_by_shifts(part, axis):
    count = lax.psum(1, axis)
    me = lax.axis_index(axis)
    received = [part]
    for shift in range(1, count):
        pairs = [(src, (src + shift) % count) for src in range(count)]
        received.append(lax.ppermute(part, axis, pairs))
    stacked = jnp.stack(received)
    order = (me - jnp.arange(count, dtype=jnp.int32)) % count
    return jnp.take(stacked, order, axis=0).reshape(-1)


def per_device(
    tokens,
    segment,
    attn_gain,
    w_query,
    w_key,
    w_value,
    q_gain,
    k_gain,
    w_out,
    ffn_gain,
    w_gate,
    w_up,
    w_down,
):
    shard_rows = tokens.shape[0]
    groups = H // KVH
    row_base = lax.axis_index("hid") * shard_rows
    group_seg = gather_by_shifts(segment, "hid")
    positions = lax.dynamic_slice_in_dim(seg_positions(group_seg), row_base, shard_rows)
    query_idx = row_base + jnp.arange(shard_rows, dtype=jnp.int32)
    seg_start = query_idx - positions
    resid = tokens.astype(jnp.float32)
    normed = rms_scale(resid, attn_gain).astype(jnp.bfloat16)
    q_raw = jnp.dot(normed, w_query, preferred_element_type=jnp.float32).reshape(shard_rows, H, HD)
    k_raw = jnp.dot(normed, w_key, preferred_element_type=jnp.float32).reshape(shard_rows, KVH, HD)
    queries = rotate(rms_scale(q_raw, q_gain), positions).astype(jnp.bfloat16)
    key_heads = (
        rotate(rms_scale(k_raw, k_gain), positions)
        .astype(jnp.bfloat16)
        .reshape(shard_rows, KVH * HD)
    )
    values = jnp.dot(normed, w_value, preferred_element_type=jnp.float32).astype(jnp.bfloat16)
    kv_cache = jnp.concatenate([key_heads, values], axis=1)
    q_grid = queries.reshape(shard_rows, KVH, groups, HD).transpose(1, 2, 0, 3)
    start_state = (
        jnp.full((KVH, groups, shard_rows), NEG_FILL, jnp.float32),
        jnp.zeros((KVH, groups, shard_rows), jnp.float32),
        jnp.zeros((KVH, groups, shard_rows, HD), jnp.float32),
    )
    kv_part = lax.all_gather(kv_cache, "hid", axis=0, tiled=True)
    unit_rows = lax.all_gather(
        jnp.concatenate([w_gate, w_up, w_down], axis=1), "hid", axis=0, tiled=True
    )
    width = w_gate.shape[1]
    gate_rows = unit_rows[:, :width]
    up_rows = unit_rows[:, width : 2 * width]
    down_rows = unit_rows[:, 2 * width :]
    key_part = kv_part[:, : KVH * HD]
    val_part = kv_part[:, KVH * HD :]
    key_count = key_part.shape[0]
    blk_len = block_length(shard_rows)

    def one_block(block_idx, state_in):
        offset = jnp.asarray(block_idx, jnp.int32) * blk_len
        local_off = jnp.asarray(block_idx, jnp.int32) * blk_len
        key_blk = lax.dynamic_slice_in_dim(key_part, local_off, blk_len)
        val_blk = lax.dynamic_slice_in_dim(val_part, local_off, blk_len)
        key_idx = offset + jnp.arange(blk_len, dtype=jnp.int32)
        return key_block(state_in, key_blk, val_blk, key_idx, q_grid, seg_start, query_idx)

    run_peak, run_total, run_acc = lax.fori_loop(0, key_count // blk_len, one_block, start_state)
    attended = (
        (run_acc / run_total[..., None])
        .transpose(2, 0, 1, 3)
        .reshape(shard_rows, H * HD)
        .astype(jnp.bfloat16)
    )
    after_attn = (resid + jnp.dot(attended, w_out, preferred_element_type=jnp.float32)).astype(
        jnp.bfloat16
    )
    after_f32 = lax.optimization_barrier(after_attn).astype(jnp.float32)
    mlp_in = rms_scale(after_f32, ffn_gain).astype(jnp.bfloat16)
    gathered = lax.all_gather(mlp_in, "req", axis=0, tiled=True)
    unit_sum = unit_terms((gate_rows, up_rows, down_rows), gathered)
    own_share = lax.psum_scatter(
        unit_sum.astype(jnp.bfloat16), "req", scatter_dimension=0, tiled=True
    ).astype(jnp.float32)
    mixed = (after_f32 + own_share).astype(jnp.bfloat16)
    return (mixed, kv_cache)


def solution(mesh):
    placed = (
        P(("req", "hid"), None),
        P(("req", "hid")),
        P(),
        P(),
        P(),
        P(),
        P(),
        P(),
        P(),
        P(),
        P(("req", "hid"), None),
        P(("req", "hid"), None),
        P(("req", "hid"), None),
    )
    return jax.shard_map(
        per_device,
        mesh=mesh,
        in_specs=placed,
        out_specs=(P(("req", "hid"), None), P(("req", "hid"), None)),
        check_vma=False,
    )
```

profile of v0, /device:TPU:0, one launch (start us, length us, event | category | flops | bytes accessed | tf_op | source)
XLA Modules:
  0.0 325.9 jit_solution(5350931809723681569)
XLA Ops:
  7.2 2.1 collective-permute-start
  9.3 6.0 %collective-permute-start.9 = (s32[192]{0:T(256)}, s32[192]{0:T(256)S(1)}, u32[]{:S(2)}, u32[]{:S(2)}) collective-permute-start(s32[192]{0:T(256)} %param.16), channel_id=1, source_target_pairs={{0,10},{1,11},{2,12},{3,13},{4,14},{5,15},{6,0},{7,1},{8,2},{9,3},... | collective-permute-start | bytes 2312 | tf_op jit(solution)/shard_map/ppermute | solution.py:79
  17.5 2.0 collective-permute-start.12
  24.2 2.5 collective-permute-start.14
  26.7 2.7 collective-permute-start.1
  32.0 3.3 %collective-permute-start.5 = (s32[192]{0:T(256)S(1)}, s32[192]{0:T(256)S(1)}, u32[]{:S(2)}, u32[]{:S(2)}) collective-permute-start(s32[192]{0:T(256)S(1)} %copy-done.7), channel_id=1, source_target_pairs={{0,6},{1,7},{2,8},{3,9},{4,10},{5,11},{6,12},{7,13},{8,14},{9,15},... | collective-permute-start | bytes 2312 | tf_op jit(solution)/shard_map/ppermute | solution.py:79
  35.3 1.9 collective-permute-start.6
  37.2 2.7 collective-permute-start.7
  42.3 3.3 %collective-permute-done.8 = s32[192]{0:T(256)S(1)} collective-permute-done((s32[192]{0:T(256)S(1)}, s32[192]{0:T(256)S(1)}, u32[]{:S(2)}, u32[]{:S(2)}) %collective-permute-start.8) | collective-permute-done | bytes 800 | tf_op jit(solution)/shard_map/ppermute | solution.py:79
  49.7 4.3 %fusion.34 = f32[192,1536]{0,1:T(8,128)S(1)} fusion(bf16[1536,1536]{1,0:T(8,128)(2,1)} %param.18, bf16[192,1536]{1,0:T(8,128)(2,1)S(1)} %copy-done.2, f32[1536]{0:T(1024)S(1)} %copy-done.11, f32[192]{0:T(256)S(1)} %add_rsqrt_fusion.3), kind=kOutput, calls=%fused_computation.87 | convolution fusion | flops 907149312 | bytes 6494976 | tf_op jit(solution)/shard_map/dot_general | solution.py:109
  55.0 56.3 %all-gather.5.cloned.1.call-done = bf16[3072,1024]{1,0:T(8,128)(2,1)} async-done(((bf16[192,1024]{1,0:T(8,128)(2,1)}), bf16[3072,1024]{1,0:T(8,128)(2,1)}) %all-gather.5.cloned.1.call-update) | async-done | bytes 6291472 | tf_op jit(solution)/shard_map/all_gather | solution.py:125
  111.3 5.9 %fusion.39 = (bf16[3072,512]{1,0:T(8,128)(2,1)}, bf16[3072,512]{1,0:T(8,128)(2,1)}) fusion(bf16[3072,1024]{1,0:T(8,128)(2,1)} %all-gather.5.cloned.1.call-done), kind=kLoop, calls=%fused_computation.89 | loop fusion | bytes 12582912 | tf_op jit(solution)/shard_map/slice | solution.py:134
  117.3 98.7 %while.18 = (s32[]{:T(128)}, f32[8,3,192]{2,1,0:T(4,128)S(1)}, f32[8,3,192]{2,1,0:T(4,128)S(1)}, f32[8,3,192,64]{2,3,1,0:T(8,128)}, s32[192]{0:T(256)S(1)}, /*in...) while((s32[]{:T(128)}, f32[8,3,192]{2,1,0:T(4,128)S(1)}, ...), condition=%wide.region_8.9_spmd.clone, body=%wide.region_5.8_spmd.clone.sunk | while | flops 953327040 | bytes 54174144 | solution.py:146
  119.2 6.6 %fusion.62 = (f32[8,3,192]{2,1,0:T(4,128)S(1)}, f32[8,768,3,192]{1,3,2,0:T(8,128)}) fusion(pred[192,768]{1,0:T(8,128)(4,1)S(1)} %compare_and_fusion.3, bf16[8,768,64,1]{1,2,3,0:T(8,128)(2,1)S(1)} %bitcast.91, bf16[8,3,192,64]{2,3,1,0:T(8,128)(2,1)S(1)} %get-tuple-element.354), kind=kOutput, calls=%fused_computation.4.clone.1 | convolution fusion | flops 463597056 | bytes 15697920 | tf_op jit(solution)/shard_map/while/body/eval_jaxpr/kgqd,kcd->kgqc/dot_general | solution.py:49
  125.9 7.6 %fusion.63 = f32[8,3,192]{2,1,0:T(4,128)S(1)} fusion(f32[8,768,3,192]{1,3,2,0:T(8,128)} %get-tuple-element.318, f32[8,3,192]{2,1,0:T(4,128)S(1)} %select_maximum_fusion.2, pred[192,768]{1,0:T(8,128)(4,1)S(1)} %compare_and_fusion.3), kind=kLoop, calls=%fused_computation.6.clone.1 | loop fusion | flops 17690112 | bytes 14340096 | tf_op jit(solution)/shard_map/while/body/eval_jaxpr/reduce_sum | solution.py:57
  133.8 8.0 %fusion.65 = f32[8,3,192,64]{2,3,1,0:T(8,128)} fusion(f32[8,3,192,64]{2,3,1,0:T(8,128)} %get-tuple-element.338, bf16[8,768,64,1]{1,2,3,0:T(8,128)(2,1)S(1)} %bitcast.92, f32[8,768,3,192]{1,3,2,0:T(8,128)} %get-tuple-element.318, f32[8,3,192]{2,1,0:T(4,128)S(1)} %select_maximum_fusion.2, pred[192,768]{1,0:T(8,128)(4,1)S(1)} %compare_and_fusion.3, ...), kind=kOutput, calls=%fused_computation.10.clone.1 | convolution fusion | flops 471564288 | bytes 17485824 | tf_op jit(solution)/shard_map/while/body/eval_jaxpr/kgqc,kcd->kgqd/dot_general | solution.py:58
  143.8 6.4 %fusion.62 = (f32[8,3,192]{2,1,0:T(4,128)S(1)}, f32[8,768,3,192]{1,3,2,0:T(8,128)}) fusion(pred[192,768]{1,0:T(8,128)(4,1)S(1)} %compare_and_fusion.3, bf16[8,768,64,1]{1,2,3,0:T(8,128)(2,1)S(1)} %bitcast.91, bf16[8,3,192,64]{2,3,1,0:T(8,128)(2,1)S(1)} %get-tuple-element.354), kind=kOutput, calls=%fused_computation.4.clone.1 | convolution fusion | flops 463597056 | bytes 15697920 | tf_op jit(solution)/shard_map/while/body/eval_jaxpr/kgqd,kcd->kgqc/dot_general | solution.py:49
  150.2 7.8 %fusion.63 = f32[8,3,192]{2,1,0:T(4,128)S(1)} fusion(f32[8,768,3,192]{1,3,2,0:T(8,128)} %get-tuple-element.318, f32[8,3,192]{2,1,0:T(4,128)S(1)} %select_maximum_fusion.2, pred[192,768]{1,0:T(8,128)(4,1)S(1)} %compare_and_fusion.3), kind=kLoop, calls=%fused_computation.6.clone.1 | loop fusion | flops 17690112 | bytes 14340096 | tf_op jit(solution)/shard_map/while/body/eval_jaxpr/reduce_sum | solution.py:57
  158.3 8.5 %fusion.65 = f32[8,3,192,64]{2,3,1,0:T(8,128)} fusion(f32[8,3,192,64]{2,3,1,0:T(8,128)} %get-tuple-element.338, bf16[8,768,64,1]{1,2,3,0:T(8,128)(2,1)S(1)} %bitcast.92, f32[8,768,3,192]{1,3,2,0:T(8,128)} %get-tuple-element.318, f32[8,3,192]{2,1,0:T(4,128)S(1)} %select_maximum_fusion.2, pred[192,768]{1,0:T(8,128)(4,1)S(1)} %compare_and_fusion.3, ...), kind=kOutput, calls=%fused_computation.10.clone.1 | convolution fusion | flops 471564288 | bytes 17485824 | tf_op jit(solution)/shard_map/while/body/eval_jaxpr/kgqc,kcd->kgqd/dot_general | solution.py:58
  168.8 6.4 %fusion.62 = (f32[8,3,192]{2,1,0:T(4,128)S(1)}, f32[8,768,3,192]{1,3,2,0:T(8,128)}) fusion(pred[192,768]{1,0:T(8,128)(4,1)S(1)} %compare_and_fusion.3, bf16[8,768,64,1]{1,2,3,0:T(8,128)(2,1)S(1)} %bitcast.91, bf16[8,3,192,64]{2,3,1,0:T(8,128)(2,1)S(1)} %get-tuple-element.354), kind=kOutput, calls=%fused_computation.4.clone.1 | convolution fusion | flops 463597056 | bytes 15697920 | tf_op jit(solution)/shard_map/while/body/eval_jaxpr/kgqd,kcd->kgqc/dot_general | solution.py:49
  175.2 7.6 %fusion.63 = f32[8,3,192]{2,1,0:T(4,128)S(1)} fusion(f32[8,768,3,192]{1,3,2,0:T(8,128)} %get-tuple-element.318, f32[8,3,192]{2,1,0:T(4,128)S(1)} %select_maximum_fusion.2, pred[192,768]{1,0:T(8,128)(4,1)S(1)} %compare_and_fusion.3), kind=kLoop, calls=%fused_computation.6.clone.1 | loop fusion | flops 17690112 | bytes 14340096 | tf_op jit(solution)/shard_map/while/body/eval_jaxpr/reduce_sum | solution.py:57
  183.1 8.3 %fusion.65 = f32[8,3,192,64]{2,3,1,0:T(8,128)} fusion(f32[8,3,192,64]{2,3,1,0:T(8,128)} %get-tuple-element.338, bf16[8,768,64,1]{1,2,3,0:T(8,128)(2,1)S(1)} %bitcast.92, f32[8,768,3,192]{1,3,2,0:T(8,128)} %get-tuple-element.318, f32[8,3,192]{2,1,0:T(4,128)S(1)} %select_maximum_fusion.2, pred[192,768]{1,0:T(8,128)(4,1)S(1)} %compare_and_fusion.3, ...), kind=kOutput, calls=%fused_computation.10.clone.1 | convolution fusion | flops 471564288 | bytes 17485824 | tf_op jit(solution)/shard_map/while/body/eval_jaxpr/kgqc,kcd->kgqd/dot_general | solution.py:58
  193.4 6.4 %fusion.62 = (f32[8,3,192]{2,1,0:T(4,128)S(1)}, f32[8,768,3,192]{1,3,2,0:T(8,128)}) fusion(pred[192,768]{1,0:T(8,128)(4,1)S(1)} %compare_and_fusion.3, bf16[8,768,64,1]{1,2,3,0:T(8,128)(2,1)S(1)} %bitcast.91, bf16[8,3,192,64]{2,3,1,0:T(8,128)(2,1)S(1)} %get-tuple-element.354), kind=kOutput, calls=%fused_computation.4.clone.1 | convolution fusion | flops 463597056 | bytes 15697920 | tf_op jit(solution)/shard_map/while/body/eval_jaxpr/kgqd,kcd->kgqc/dot_general | solution.py:49
  199.8 7.6 %fusion.63 = f32[8,3,192]{2,1,0:T(4,128)S(1)} fusion(f32[8,768,3,192]{1,3,2,0:T(8,128)} %get-tuple-element.318, f32[8,3,192]{2,1,0:T(4,128)S(1)} %select_maximum_fusion.2, pred[192,768]{1,0:T(8,128)(4,1)S(1)} %compare_and_fusion.3), kind=kLoop, calls=%fused_computation.6.clone.1 | loop fusion | flops 17690112 | bytes 14340096 | tf_op jit(solution)/shard_map/while/body/eval_jaxpr/reduce_sum | solution.py:57
  207.7 8.3 %fusion.65 = f32[8,3,192,64]{2,3,1,0:T(8,128)} fusion(f32[8,3,192,64]{2,3,1,0:T(8,128)} %get-tuple-element.338, bf16[8,768,64,1]{1,2,3,0:T(8,128)(2,1)S(1)} %bitcast.92, f32[8,768,3,192]{1,3,2,0:T(8,128)} %get-tuple-element.318, f32[8,3,192]{2,1,0:T(4,128)S(1)} %select_maximum_fusion.2, pred[192,768]{1,0:T(8,128)(4,1)S(1)} %compare_and_fusion.3, ...), kind=kOutput, calls=%fused_computation.10.clone.1 | convolution fusion | flops 471564288 | bytes 17485824 | tf_op jit(solution)/shard_map/while/body/eval_jaxpr/kgqc,kcd->kgqd/dot_general | solution.py:58
  217.6 3.6 %fusion.15 = bf16[192,1536]{1,0:T(8,128)(2,1)S(1)} fusion(bf16[192,1536]{0,1:T(8,128)(2,1)S(1)} %bitcast.98, bf16[1536,1536]{1,0:T(8,128)(2,1)} %param.23, bf16[192,1536]{1,0:T(8,128)(2,1)} %param.15), kind=kOutput, calls=%fused_computation.26 | convolution fusion | flops 906854400 | bytes 6488064 | tf_op jit(solution)/shard_map/dot_general | solution.py:153
  222.8 7.7 %reshape.217 = bf16[576,4608]{1,0:T(8,128)(2,1)} reshape(bf16[16,36,4608]{2,1,0:T(8,128)(2,1)} %all-gather.9.cloned.1.call-done) | data formatting | bytes 10616832
  230.5 26.2 %all-gather.7.cloned.1.call-done = bf16[1536,1536]{1,0:T(8,128)(2,1)} async-done(((bf16[192,1536]{1,0:T(8,128)(2,1)}), bf16[1536,1536]{1,0:T(8,128)(2,1)}) %all-gather.7.cloned.1.call-update) | async-done | bytes 4718608 | tf_op jit(solution)/shard_map/all_gather | solution.py:158
  256.7 7.6 %fusion.18 = f32[1536,576]{0,1:T(8,128)} fusion(bf16[1536,1536]{1,0:T(8,128)(2,1)} %all-gather.7.cloned.1.call-done, bf16[576,4608]{1,0:T(8,128)(2,1)} %reshape.217), kind=kOutput, calls=%fused_computation.29 | convolution fusion | flops 2717908992 | bytes 10027008 | tf_op jit(solution)/shard_map/dot_general | solution.py:67
  264.4 13.8 %convolution_convert_fusion = bf16[1536,1536]{1,0:T(8,128)(2,1)} fusion(bf16[576,4608]{1,0:T(8,128)(2,1)} %reshape.217, f32[1536,576]{0,1:T(8,128)} %fusion.18, bf16[1536,1536]{1,0:T(8,128)(2,1)} %all-gather.7.cloned.1.call-done), kind=kOutput, calls=%fused_computation.23 | convolution fusion | flops 5443485696 | bytes 16515072 | tf_op jit(solution)/shard_map/dot_general | solution.py:70
  278.2 39.2 %reduce-scatter.2.cloned.1.call-done = bf16[192,1536]{1,0:T(8,128)(2,1)} async-done(((bf16[1536,1536]{1,0:T(8,128)(2,1)}), bf16[192,1536]{1,0:T(8,128)(2,1)}) %reduce-scatter.2.cloned.1.call-update) | async-done | bytes 589840 | tf_op jit(solution)/shard_map/reduce_scatter | solution.py:160
  317.4 2.0 fusion.28
  (130 shorter events, 28.8 us)
Async XLA Ops:
  7.2 13.7 %copy-start = (bf16[1536,512]{1,0:T(8,128)(2,1)S(1)}, bf16[1536,512]{1,0:T(8,128)(2,1)}, u32[]{:S(2)}) copy-start(bf16[1536,512]{1,0:T(8,128)(2,1)} %param.19) | copy-start | bytes 4718596
  7.2 15.6 %copy-start.2 = (bf16[192,1536]{1,0:T(8,128)(2,1)S(1)}, bf16[192,1536]{1,0:T(8,128)(2,1)}, u32[]{:S(2)}) copy-start(bf16[192,1536]{1,0:T(8,128)(2,1)} %param.15) | copy-start | bytes 1769476
  7.2 15.6 %copy-start.11 = (f32[1536]{0:T(1024)S(1)}, f32[1536]{0:T(1024)}, u32[]{:S(2)}) copy-start(f32[1536]{0:T(1024)} %param.17) | copy-start | bytes 18436
  7.2 104.1 %all-gather.5.cloned.1.call-start = ((), (), s32[]{:S(2)}) async-start(), calls=%async_computation.1 | async-start | bytes 6684672 | tf_op jit(solution)/shard_map/all_gather | solution.py:125
  7.2 16.3 %collective-permute-start = (s32[192]{0:T(256)}, s32[192]{0:T(256)S(1)}, u32[]{:S(2)}, u32[]{:S(2)}) collective-permute-start(s32[192]{0:T(256)} %param.16), channel_id=1, source_target_pairs={{0,1},{1,2},{2,3},{3,4},{4,5},{5,6},{6,7},{7,8},{8,9},{9,10},{10,1... | collective-permute-start | bytes 2312 | tf_op jit(solution)/shard_map/ppermute | solution.py:79
  9.3 14.9 %collective-permute-start.9 = (s32[192]{0:T(256)}, s32[192]{0:T(256)S(1)}, u32[]{:S(2)}, u32[]{:S(2)}) collective-permute-start(s32[192]{0:T(256)} %param.16), channel_id=1, source_target_pairs={{0,10},{1,11},{2,12},{3,13},{4,14},{5,15},{6,0},{7,1},{8,2},{9,3},... | collective-permute-start | bytes 2312 | tf_op jit(solution)/shard_map/ppermute | solution.py:79
  15.4 11.3 %collective-permute-start.10 = (s32[192]{0:T(256)}, s32[192]{0:T(256)S(1)}, u32[]{:S(2)}, u32[]{:S(2)}) collective-permute-start(s32[192]{0:T(256)} %param.16), channel_id=1, source_target_pairs={{0,11},{1,12},{2,13},{3,14},{4,15},{5,0},{6,1},{7,2},{8,3},{9,4},{... | collective-permute-start | bytes 2312 | tf_op jit(solution)/shard_map/ppermute | solution.py:79
  16.3 13.1 %collective-permute-start.11 = (s32[192]{0:T(256)}, s32[192]{0:T(256)S(1)}, u32[]{:S(2)}, u32[]{:S(2)}) collective-permute-start(s32[192]{0:T(256)} %param.16), channel_id=1, source_target_pairs={{0,12},{1,13},{2,14},{3,15},{4,0},{5,1},{6,2},{7,3},{8,4},{9,5},{1... | collective-permute-start | bytes 2312 | tf_op jit(solution)/shard_map/ppermute | solution.py:79
  17.5 11.9 %collective-permute-start.12 = (s32[192]{0:T(256)}, s32[192]{0:T(256)S(1)}, u32[]{:S(2)}, u32[]{:S(2)}) collective-permute-start(s32[192]{0:T(256)} %param.16), channel_id=1, source_target_pairs={{0,13},{1,14},{2,15},{3,0},{4,1},{5,2},{6,3},{7,4},{8,5},{9,6},{10... | collective-permute-start | bytes 2312 | tf_op jit(solution)/shard_map/ppermute | solution.py:79
  19.5 3.3 %copy-start.10 = (bf16[1536,512]{1,0:T(8,128)(2,1)S(1)}, bf16[1536,512]{1,0:T(8,128)(2,1)}, u32[]{:S(2)}) copy-start(bf16[1536,512]{1,0:T(8,128)(2,1)} %param.20) | copy-start | bytes 4718596
  20.9 2.5 copy-start.8
  20.9 2.7 copy-start.7
  22.8 25.8 %copy-start.3 = (bf16[36,1536]{1,0:T(8,128)(2,1)S(1)}, bf16[36,1536]{1,0:T(8,128)(2,1)}, u32[]{:S(2)}) copy-start(bf16[36,1536]{1,0:T(8,128)(2,1)} %param.27) | copy-start | bytes 331780
  22.8 25.8 %copy-start.4 = (bf16[36,1536]{1,0:T(8,128)(2,1)S(1)}, bf16[36,1536]{1,0:T(8,128)(2,1)}, u32[]{:S(2)}) copy-start(bf16[36,1536]{1,0:T(8,128)(2,1)} %param.26) | copy-start | bytes 331780
  22.8 25.8 %copy-start.5 = (bf16[36,1536]{1,0:T(8,128)(2,1)S(1)}, bf16[36,1536]{1,0:T(8,128)(2,1)}, u32[]{:S(2)}) copy-start(bf16[36,1536]{1,0:T(8,128)(2,1)} %param.25) | copy-start | bytes 331780
  23.6 6.7 %collective-permute-start.13 = (s32[192]{0:T(256)S(1)}, s32[192]{0:T(256)S(1)}, u32[]{:S(2)}, u32[]{:S(2)}) collective-permute-start(s32[192]{0:T(256)S(1)} %copy-done.7), channel_id=1, source_target_pairs={{0,14},{1,15},{2,0},{3,1},{4,2},{5,3},{6,4},{7,5},{8,6},{9,7},{10,... | collective-permute-start | bytes 2312 | tf_op jit(solution)/shard_map/ppermute | solution.py:79
  24.2 7.8 %collective-permute-start.14 = (s32[192]{0:T(256)S(1)}, s32[192]{0:T(256)S(1)}, u32[]{:S(2)}, u32[]{:S(2)}) collective-permute-start(s32[192]{0:T(256)S(1)} %copy-done.7), channel_id=1, source_target_pairs={{0,15},{1,0},{2,1},{3,2},{4,3},{5,4},{6,5},{7,6},{8,7},{9,8},{10,9... | collective-permute-start | bytes 2312 | tf_op jit(solution)/shard_map/ppermute | solution.py:79
  26.7 8.7 %collective-permute-start.1 = (s32[192]{0:T(256)S(1)}, s32[192]{0:T(256)S(1)}, u32[]{:S(2)}, u32[]{:S(2)}) collective-permute-start(s32[192]{0:T(256)S(1)} %copy-done.7), channel_id=1, source_target_pairs={{0,2},{1,3},{2,4},{3,5},{4,6},{5,7},{6,8},{7,9},{8,10},{9,11},{10,... | collective-permute-start | bytes 2312 | tf_op jit(solution)/shard_map/ppermute | solution.py:79
  29.4 7.8 %collective-permute-start.2 = (s32[192]{0:T(256)S(1)}, s32[192]{0:T(256)S(1)}, u32[]{:S(2)}, u32[]{:S(2)}) collective-permute-start(s32[192]{0:T(256)S(1)} %copy-done.7), channel_id=1, source_target_pairs={{0,3},{1,4},{2,5},{3,6},{4,7},{5,8},{6,9},{7,10},{8,11},{9,12},{10... | collective-permute-start | bytes 2312 | tf_op jit(solution)/shard_map/ppermute | solution.py:79
  29.4 10.5 %collective-permute-start.3 = (s32[192]{0:T(256)S(1)}, s32[192]{0:T(256)S(1)}, u32[]{:S(2)}, u32[]{:S(2)}) collective-permute-start(s32[192]{0:T(256)S(1)} %copy-done.7), channel_id=1, source_target_pairs={{0,4},{1,5},{2,6},{3,7},{4,8},{5,9},{6,10},{7,11},{8,12},{9,13},{1... | collective-permute-start | bytes 2312 | tf_op jit(solution)/shard_map/ppermute | solution.py:79
  30.3 11.5 %collective-permute-start.4 = (s32[192]{0:T(256)S(1)}, s32[192]{0:T(256)S(1)}, u32[]{:S(2)}, u32[]{:S(2)}) collective-permute-start(s32[192]{0:T(256)S(1)} %copy-done.7), channel_id=1, source_target_pairs={{0,5},{1,6},{2,7},{3,8},{4,9},{5,10},{6,11},{7,12},{8,13},{9,14},{... | collective-permute-start | bytes 2312 | tf_op jit(solution)/shard_map/ppermute | solution.py:79
  32.0 9.8 %collective-permute-start.5 = (s32[192]{0:T(256)S(1)}, s32[192]{0:T(256)S(1)}, u32[]{:S(2)}, u32[]{:S(2)}) collective-permute-start(s32[192]{0:T(256)S(1)} %copy-done.7), channel_id=1, source_target_pairs={{0,6},{1,7},{2,8},{3,9},{4,10},{5,11},{6,12},{7,13},{8,14},{9,15},... | collective-permute-start | bytes 2312 | tf_op jit(solution)/shard_map/ppermute | solution.py:79
  35.3 6.5 %collective-permute-start.6 = (s32[192]{0:T(256)S(1)}, s32[192]{0:T(256)S(1)}, u32[]{:S(2)}, u32[]{:S(2)}) collective-permute-start(s32[192]{0:T(256)S(1)} %copy-done.7), channel_id=1, source_target_pairs={{0,7},{1,8},{2,9},{3,10},{4,11},{5,12},{6,13},{7,14},{8,15},{9,0},... | collective-permute-start | bytes 2312 | tf_op jit(solution)/shard_map/ppermute | solution.py:79
  37.2 5.1 %collective-permute-start.7 = (s32[192]{0:T(256)S(1)}, s32[192]{0:T(256)S(1)}, u32[]{:S(2)}, u32[]{:S(2)}) collective-permute-start(s32[192]{0:T(256)S(1)} %copy-done.7), channel_id=1, source_target_pairs={{0,8},{1,9},{2,10},{3,11},{4,12},{5,13},{6,14},{7,15},{8,0},{9,1},... | collective-permute-start | bytes 2312 | tf_op jit(solution)/shard_map/ppermute | solution.py:79
  39.9 5.7 %collective-permute-start.8 = (s32[192]{0:T(256)S(1)}, s32[192]{0:T(256)S(1)}, u32[]{:S(2)}, u32[]{:S(2)}) collective-permute-start(s32[192]{0:T(256)S(1)} %copy-done.7), channel_id=1, source_target_pairs={{0,9},{1,10},{2,11},{3,12},{4,13},{5,14},{6,15},{7,0},{8,1},{9,2},... | collective-permute-start | bytes 2312 | tf_op jit(solution)/shard_map/ppermute | solution.py:79
  48.5 174.2 %all-gather.9.cloned.1.call-start = ((), (), s32[]{:S(2)}) async-start(), calls=%async_computation.4 | async-start | bytes 6266880 | tf_op jit(solution)/shard_map/all_gather | solution.py:126
  49.4 207.3 %all-gather.7.cloned.1.call-start = ((), (), s32[]{:S(2)}) async-start(), calls=%async_computation.2 | async-start | bytes 5308416 | tf_op jit(solution)/shard_map/all_gather | solution.py:158
  49.7 4.6 %copy-start.9 = (f32[64]{0:T(128)S(1)}, f32[64]{0:T(128)}, u32[]{:S(2)}) copy-start(f32[64]{0:T(128)} %param.21) | copy-start | bytes 772
  217.6 3.8 %copy-start.6 = (f32[1536]{0:T(1024)S(1)}, f32[1536]{0:T(1024)}, u32[]{:S(2)}) copy-start(f32[1536]{0:T(1024)} %param.24) | copy-start | bytes 18436
  222.5 94.9 %reduce-scatter.2.cloned.1.call-start = ((), (), s32[]{:S(2)}) async-start(), calls=%async_computation.3 | async-start | bytes 5308416 | tf_op jit(solution)/shard_map/reduce_scatter | solution.py:160
  278.2 41.2 %copy-start.1 = (bf16[1536,512]{1,0:T(8,128)(2,1)S(1)}, bf16[1536,512]{1,0:T(8,128)(2,1)}, u32[]{:S(2)}) copy-start(bf16[1536,512]{1,0:T(8,128)(2,1)} %param.19) | copy-start | bytes 4718596
Sparse Core Ops, SparseCore 0:
  48.7 62.6 all-gather.4
  113.5 59.1 all-gather.8
  222.6 34.0 all-gather.6
  278.3 39.0 reduce-scatter.1
where the time goes:
time: 327 us; the launch traced here: 326 us
  waiting for transfers between devices  126 us (39%)
  matrix products  90.6 us (28%)
  other arithmetic  41.4 us (13%)
  starting transfers between devices  31 us (9%)
  local copies, waits for them, and re-layouts  22.9 us (7%)
  between operations  14.1 us (4%)
    all_gather x1, waiting for transfers between devices, per_device(): kv_part = lax.all_gather(kv_cache, 'hid', axis=0, tiled=True)  56.3 us
    reduce_scatter x1, waiting for transfers between devices, per_device(): lax.psum_scatter(unit_sum.astype(jnp.bfloat16), 'req', scatter_dimension=...  39.2 us
    dot_general x4, matrix products, key_block(): jnp.einsum('kgqc,kcd->kgqd', weights.astype(jnp.bfloat16), v_grid, prefer...  33 us
    reduce_sum x4, other arithmetic, key_block(): new_total = run_total * factor + jnp.sum(weights, axis=-1)  30.5 us
    ppermute x15, starting transfers between devices, gather_by_shifts(): received.append(lax.ppermute(part, axis, pairs))  30.4 us
    all_gather x1, waiting for transfers between devices, per_device(): gathered = lax.all_gather(mlp_in, 'req', axis=0, tiled=True)  26.2 us
    dot_general x4, matrix products, key_block(): jnp.einsum('kgqd,kcd->kgqc', q_grid, k_grid, preferred_element_type=jnp.f...  25.8 us
    dot_general x1, matrix products, unit_terms(): return jnp.dot(hidden, down_part, preferred_element_type=jnp.float32)  13.8 us
  transfers between devices with their start and end apart: 19, of which 5 were waited for; matrix products, arithmetic and copies ran while one was open for 39% of the time, Pallas kernels for 0%

commit v1 on v0

--- a/solution.py
+++ b/solution.py
@@ -155,7 +155,9 @@
     )
     after_f32 = lax.optimization_barrier(after_attn).astype(jnp.float32)
     mlp_in = rms_scale(after_f32, ffn_gain).astype(jnp.bfloat16)
-    gathered = lax.all_gather(mlp_in, "req", axis=0, tiled=True)
+    gathered = jnp.concatenate(
+        lax.all_to_all(jnp.stack([mlp_in] * lax.axis_size("req")), "req", 0, 0), axis=0
+    )
     unit_sum = unit_terms((gate_rows, up_rows, down_rows), gathered)
     own_share = lax.psum_scatter(
         unit_sum.astype(jnp.bfloat16), "req", scatter_dimension=0, tiled=True

time: 327 us -> 352 us (1.076)
  waiting for transfers between devices: 126 us -> 145 us
  starting transfers between devices: 31 us -> 35.5 us
    all_to_all x0 -> x1, waiting for transfers between devices: none -> 47.3 us  [per_device(): lax.all_to_all(jnp.stack([mlp_in] * lax.axis_size('req')), 'req', 0, 0)]
    all_gather x1 -> x0, waiting for transfers between devices: 26.2 us -> none  [per_device(): gathered = lax.all_gather(mlp_in, 'req', axis=0, tiled=True)]
    all_to_all x0 -> x1, starting transfers between devices: none -> 4.6 us  [per_device(): lax.all_to_all(jnp.stack([mlp_in] * lax.axis_size('req')), 'req', 0, 0)]
  transfers between devices with their start and end apart: 19 -> 19, of which waited for: 5 -> 5; matrix products, arithmetic and copies ran while one was open for 39% -> 37% of each run, Pallas kernels for 0% -> 0%
where the time goes in v1:
time: 352 us; the launch traced here: 351 us
  waiting for transfers between devices  145 us (41%)
  matrix products  90.7 us (26%)
  other arithmetic  40.6 us (12%)
  starting transfers between devices  35.5 us (10%)
  local copies, waits for them, and re-layouts  25.4 us (7%)
  between operations  14.1 us (4%)
    all_gather x1, waiting for transfers between devices, per_device(): kv_part = lax.all_gather(kv_cache, 'hid', axis=0, tiled=True)  56.4 us
    all_to_all x1, waiting for transfers between devices, per_device(): lax.all_to_all(jnp.stack([mlp_in] * lax.axis_size('req')), 'req', 0, 0)  47.3 us
    reduce_scatter x1, waiting for transfers between devices, per_device(): lax.psum_scatter(unit_sum.astype(jnp.bfloat16), 'req', scatter_dimension=...  37.2 us
    dot_general x4, matrix products, key_block(): jnp.einsum('kgqc,kcd->kgqd', weights.astype(jnp.bfloat16), v_grid, prefer...  33.1 us
    reduce_sum x4, other arithmetic, key_block(): new_total = run_total * factor + jnp.sum(weights, axis=-1)  30.5 us
    ppermute x15, starting transfers between devices, gather_by_shifts(): received.append(lax.ppermute(part, axis, pairs))  30.4 us
    dot_general x4, matrix products, key_block(): jnp.einsum('kgqd,kcd->kgqc', q_grid, k_grid, preferred_element_type=jnp.f...  25.8 us
    dot_general x1, matrix products, unit_terms(): return jnp.dot(hidden, down_part, preferred_element_type=jnp.float32)  13.8 us
  transfers between devices with their start and end apart: 19, of which 5 were waited for; matrix products, arithmetic and copies ran while one was open for 37% of the time, Pallas kernels for 0%

profile of v1, /device:TPU:0, one launch (start us, length us, event | category | flops | bytes accessed | tf_op | source)
XLA Modules:
  0.0 351.3 jit_solution(17174085410016462025)
XLA Ops:
  7.2 2.1 collective-permute-start
  9.3 6.0 %collective-permute-start.9 = (s32[192]{0:T(256)}, s32[192]{0:T(256)S(1)}, u32[]{:S(2)}, u32[]{:S(2)}) collective-permute-start(s32[192]{0:T(256)} %param.16), channel_id=1, source_target_pairs={{0,10},{1,11},{2,12},{3,13},{4,14},{5,15},{6,0},{7,1},{8,2},{9,3},... | collective-permute-start | bytes 2312 | tf_op jit(solution)/shard_map/ppermute | solution.py:79
  24.2 2.5 collective-permute-start.14
  26.7 2.7 collective-permute-start.1
  32.0 3.3 collective-permute-start.5
  37.2 2.7 collective-permute-start.7
  42.3 3.3 collective-permute-done.8
  49.6 4.3 %fusion.34 = f32[192,1536]{0,1:T(8,128)S(1)} fusion(bf16[1536,1536]{1,0:T(8,128)(2,1)} %param.18, bf16[192,1536]{1,0:T(8,128)(2,1)S(1)} %copy-done.2, f32[1536]{0:T(1024)S(1)} %copy-done.11, f32[192]{0:T(256)S(1)} %add_rsqrt_fusion.3), kind=kOutput, calls=%fused_computation.87 | convolution fusion | flops 907149312 | bytes 6494976 | tf_op jit(solution)/shard_map/dot_general | solution.py:109
  54.9 56.4 %all-gather.4.cloned.1.call-done = bf16[3072,1024]{1,0:T(8,128)(2,1)} async-done(((bf16[192,1024]{1,0:T(8,128)(2,1)}), bf16[3072,1024]{1,0:T(8,128)(2,1)}) %all-gather.4.cloned.1.call-update) | async-done | bytes 6291472 | tf_op jit(solution)/shard_map/all_gather | solution.py:125
  111.3 5.9 %fusion.39 = (bf16[3072,512]{1,0:T(8,128)(2,1)}, bf16[3072,512]{1,0:T(8,128)(2,1)}) fusion(bf16[3072,1024]{1,0:T(8,128)(2,1)} %all-gather.4.cloned.1.call-done), kind=kLoop, calls=%fused_computation.89 | loop fusion | bytes 12582912 | tf_op jit(solution)/shard_map/slice | solution.py:134
  117.3 98.8 %while.18 = (s32[]{:T(128)}, f32[8,3,192]{2,1,0:T(4,128)S(1)}, f32[8,3,192]{2,1,0:T(4,128)S(1)}, f32[8,3,192,64]{2,3,1,0:T(8,128)}, s32[192]{0:T(256)S(1)}, /*in...) while((s32[]{:T(128)}, f32[8,3,192]{2,1,0:T(4,128)S(1)}, ...), condition=%wide.region_8.9_spmd.clone, body=%wide.region_5.8_spmd.clone.sunk | while | flops 953327040 | bytes 54174144 | solution.py:146
  119.2 6.6 %fusion.62 = (f32[8,3,192]{2,1,0:T(4,128)S(1)}, f32[8,768,3,192]{1,3,2,0:T(8,128)}) fusion(pred[192,768]{1,0:T(8,128)(4,1)S(1)} %compare_and_fusion.3, bf16[8,768,64,1]{1,2,3,0:T(8,128)(2,1)S(1)} %bitcast.92, bf16[8,3,192,64]{2,3,1,0:T(8,128)(2,1)S(1)} %get-tuple-element.354), kind=kOutput, calls=%fused_computation.4.clone.1 | convolution fusion | flops 463597056 | bytes 15697920 | tf_op jit(solution)/shard_map/while/body/eval_jaxpr/kgqd,kcd->kgqc/dot_general | solution.py:49
  125.9 7.7 %fusion.63 = f32[8,3,192]{2,1,0:T(4,128)S(1)} fusion(f32[8,768,3,192]{1,3,2,0:T(8,128)} %get-tuple-element.318, f32[8,3,192]{2,1,0:T(4,128)S(1)} %select_maximum_fusion.2, pred[192,768]{1,0:T(8,128)(4,1)S(1)} %compare_and_fusion.3), kind=kLoop, calls=%fused_computation.6.clone.1 | loop fusion | flops 17690112 | bytes 14340096 | tf_op jit(solution)/shard_map/while/body/eval_jaxpr/reduce_sum | solution.py:57
  133.9 8.0 %fusion.65 = f32[8,3,192,64]{2,3,1,0:T(8,128)} fusion(f32[8,3,192,64]{2,3,1,0:T(8,128)} %get-tuple-element.338, bf16[8,768,64,1]{1,2,3,0:T(8,128)(2,1)S(1)} %bitcast.93, f32[8,768,3,192]{1,3,2,0:T(8,128)} %get-tuple-element.318, f32[8,3,192]{2,1,0:T(4,128)S(1)} %select_maximum_fusion.2, pred[192,768]{1,0:T(8,128)(4,1)S(1)} %compare_and_fusion.3, ...), kind=kOutput, calls=%fused_computation.10.clone.1 | convolution fusion | flops 471564288 | bytes 17485824 | tf_op jit(solution)/shard_map/while/body/eval_jaxpr/kgqc,kcd->kgqd/dot_general | solution.py:58
  143.9 6.4 %fusion.62 = (f32[8,3,192]{2,1,0:T(4,128)S(1)}, f32[8,768,3,192]{1,3,2,0:T(8,128)}) fusion(pred[192,768]{1,0:T(8,128)(4,1)S(1)} %compare_and_fusion.3, bf16[8,768,64,1]{1,2,3,0:T(8,128)(2,1)S(1)} %bitcast.92, bf16[8,3,192,64]{2,3,1,0:T(8,128)(2,1)S(1)} %get-tuple-element.354), kind=kOutput, calls=%fused_computation.4.clone.1 | convolution fusion | flops 463597056 | bytes 15697920 | tf_op jit(solution)/shard_map/while/body/eval_jaxpr/kgqd,kcd->kgqc/dot_general | solution.py:49
  150.3 7.7 %fusion.63 = f32[8,3,192]{2,1,0:T(4,128)S(1)} fusion(f32[8,768,3,192]{1,3,2,0:T(8,128)} %get-tuple-element.318, f32[8,3,192]{2,1,0:T(4,128)S(1)} %select_maximum_fusion.2, pred[192,768]{1,0:T(8,128)(4,1)S(1)} %compare_and_fusion.3), kind=kLoop, calls=%fused_computation.6.clone.1 | loop fusion | flops 17690112 | bytes 14340096 | tf_op jit(solution)/shard_map/while/body/eval_jaxpr/reduce_sum | solution.py:57
  158.3 8.6 %fusion.65 = f32[8,3,192,64]{2,3,1,0:T(8,128)} fusion(f32[8,3,192,64]{2,3,1,0:T(8,128)} %get-tuple-element.338, bf16[8,768,64,1]{1,2,3,0:T(8,128)(2,1)S(1)} %bitcast.93, f32[8,768,3,192]{1,3,2,0:T(8,128)} %get-tuple-element.318, f32[8,3,192]{2,1,0:T(4,128)S(1)} %select_maximum_fusion.2, pred[192,768]{1,0:T(8,128)(4,1)S(1)} %compare_and_fusion.3, ...), kind=kOutput, calls=%fused_computation.10.clone.1 | convolution fusion | flops 471564288 | bytes 17485824 | tf_op jit(solution)/shard_map/while/body/eval_jaxpr/kgqc,kcd->kgqd/dot_general | solution.py:58
  168.9 6.4 %fusion.62 = (f32[8,3,192]{2,1,0:T(4,128)S(1)}, f32[8,768,3,192]{1,3,2,0:T(8,128)}) fusion(pred[192,768]{1,0:T(8,128)(4,1)S(1)} %compare_and_fusion.3, bf16[8,768,64,1]{1,2,3,0:T(8,128)(2,1)S(1)} %bitcast.92, bf16[8,3,192,64]{2,3,1,0:T(8,128)(2,1)S(1)} %get-tuple-element.354), kind=kOutput, calls=%fused_computation.4.clone.1 | convolution fusion | flops 463597056 | bytes 15697920 | tf_op jit(solution)/shard_map/while/body/eval_jaxpr/kgqd,kcd->kgqc/dot_general | solution.py:49
  175.3 7.6 %fusion.63 = f32[8,3,192]{2,1,0:T(4,128)S(1)} fusion(f32[8,768,3,192]{1,3,2,0:T(8,128)} %get-tuple-element.318, f32[8,3,192]{2,1,0:T(4,128)S(1)} %select_maximum_fusion.2, pred[192,768]{1,0:T(8,128)(4,1)S(1)} %compare_and_fusion.3), kind=kLoop, calls=%fused_computation.6.clone.1 | loop fusion | flops 17690112 | bytes 14340096 | tf_op jit(solution)/shard_map/while/body/eval_jaxpr/reduce_sum | solution.py:57
  183.2 8.3 %fusion.65 = f32[8,3,192,64]{2,3,1,0:T(8,128)} fusion(f32[8,3,192,64]{2,3,1,0:T(8,128)} %get-tuple-element.338, bf16[8,768,64,1]{1,2,3,0:T(8,128)(2,1)S(1)} %bitcast.93, f32[8,768,3,192]{1,3,2,0:T(8,128)} %get-tuple-element.318, f32[8,3,192]{2,1,0:T(4,128)S(1)} %select_maximum_fusion.2, pred[192,768]{1,0:T(8,128)(4,1)S(1)} %compare_and_fusion.3, ...), kind=kOutput, calls=%fused_computation.10.clone.1 | convolution fusion | flops 471564288 | bytes 17485824 | tf_op jit(solution)/shard_map/while/body/eval_jaxpr/kgqc,kcd->kgqd/dot_general | solution.py:58
  193.5 6.4 %fusion.62 = (f32[8,3,192]{2,1,0:T(4,128)S(1)}, f32[8,768,3,192]{1,3,2,0:T(8,128)}) fusion(pred[192,768]{1,0:T(8,128)(4,1)S(1)} %compare_and_fusion.3, bf16[8,768,64,1]{1,2,3,0:T(8,128)(2,1)S(1)} %bitcast.92, bf16[8,3,192,64]{2,3,1,0:T(8,128)(2,1)S(1)} %get-tuple-element.354), kind=kOutput, calls=%fused_computation.4.clone.1 | convolution fusion | flops 463597056 | bytes 15697920 | tf_op jit(solution)/shard_map/while/body/eval_jaxpr/kgqd,kcd->kgqc/dot_general | solution.py:49
  199.9 7.6 %fusion.63 = f32[8,3,192]{2,1,0:T(4,128)S(1)} fusion(f32[8,768,3,192]{1,3,2,0:T(8,128)} %get-tuple-element.318, f32[8,3,192]{2,1,0:T(4,128)S(1)} %select_maximum_fusion.2, pred[192,768]{1,0:T(8,128)(4,1)S(1)} %compare_and_fusion.3), kind=kLoop, calls=%fused_computation.6.clone.1 | loop fusion | flops 17690112 | bytes 14340096 | tf_op jit(solution)/shard_map/while/body/eval_jaxpr/reduce_sum | solution.py:57
  207.8 8.3 %fusion.65 = f32[8,3,192,64]{2,3,1,0:T(8,128)} fusion(f32[8,3,192,64]{2,3,1,0:T(8,128)} %get-tuple-element.338, bf16[8,768,64,1]{1,2,3,0:T(8,128)(2,1)S(1)} %bitcast.93, f32[8,768,3,192]{1,3,2,0:T(8,128)} %get-tuple-element.318, f32[8,3,192]{2,1,0:T(4,128)S(1)} %select_maximum_fusion.2, pred[192,768]{1,0:T(8,128)(4,1)S(1)} %compare_and_fusion.3, ...), kind=kOutput, calls=%fused_computation.10.clone.1 | convolution fusion | flops 471564288 | bytes 17485824 | tf_op jit(solution)/shard_map/while/body/eval_jaxpr/kgqc,kcd->kgqd/dot_general | solution.py:58
  217.7 3.6 %fusion.15 = bf16[192,1536]{1,0:T(8,128)(2,1)S(1)} fusion(bf16[192,1536]{0,1:T(8,128)(2,1)S(1)} %bitcast.99, bf16[1536,1536]{1,0:T(8,128)(2,1)} %param.23, bf16[192,1536]{1,0:T(8,128)(2,1)} %param.15), kind=kOutput, calls=%fused_computation.26 | convolution fusion | flops 906854400 | bytes 6488064 | tf_op jit(solution)/shard_map/dot_general | solution.py:153
  221.7 2.5 stack.79
  224.2 4.6 %all-to-all-start = ((bf16[8,192,1536]{2,1,0:T(8,128)(2,1)}), bf16[8,192,1536]{2,1,0:T(8,128)(2,1)}, u32[]{:S(2)}, u32[]{:S(2)}) async-start(bf16[8,192,1536]{2,1,0:T(8,128)(2,1)} %stack.79), calls=%async_computation | async-start | bytes 9437184 | tf_op jit(solution)/shard_map/all_to_all | solution.py:159
  229.1 7.7 %reshape.223 = bf16[576,4608]{1,0:T(8,128)(2,1)} reshape(bf16[16,36,4608]{2,1,0:T(8,128)(2,1)} %all-gather.6.cloned.1.call-done) | data formatting | bytes 10616832
  236.8 47.3 %all-to-all-done = bf16[8,192,1536]{2,1,0:T(8,128)(2,1)} async-done(((bf16[8,192,1536]{2,1,0:T(8,128)(2,1)}), bf16[8,192,1536]{2,1,0:T(8,128)(2,1)}, u32[]{:S(2)}, u32[]{:S(2)}) %all-to-all-start) | async-done | bytes 4718624 | tf_op jit(solution)/shard_map/all_to_all | solution.py:159
  284.1 7.6 %fusion.18 = f32[1536,576]{0,1:T(8,128)} fusion(bf16[1536,1536]{1,0:T(8,128)(2,1)} %bitcast.27, bf16[576,4608]{1,0:T(8,128)(2,1)} %reshape.223), kind=kOutput, calls=%fused_computation.29 | convolution fusion | flops 2717908992 | bytes 10027008 | tf_op jit(solution)/shard_map/dot_general | solution.py:67
  291.7 13.8 %convolution_convert_fusion = bf16[1536,1536]{1,0:T(8,128)(2,1)} fusion(bf16[576,4608]{1,0:T(8,128)(2,1)} %reshape.223, f32[1536,576]{0,1:T(8,128)} %fusion.18, bf16[1536,1536]{1,0:T(8,128)(2,1)} %bitcast.27), kind=kOutput, calls=%fused_computation.23 | convolution fusion | flops 5443485696 | bytes 16515072 | tf_op jit(solution)/shard_map/dot_general | solution.py:70
  305.6 37.2 %reduce-scatter.2.cloned.1.call-done = bf16[192,1536]{1,0:T(8,128)(2,1)} async-done(((bf16[1536,1536]{1,0:T(8,128)(2,1)}), bf16[192,1536]{1,0:T(8,128)(2,1)}) %reduce-scatter.2.cloned.1.call-update) | async-done | bytes 589840 | tf_op jit(solution)/shard_map/reduce_scatter | solution.py:162
  342.7 2.0 fusion.28
  (130 shorter events, 31.8 us)
Async XLA Ops:
  7.2 13.7 %copy-start = (bf16[1536,512]{1,0:T(8,128)(2,1)S(1)}, bf16[1536,512]{1,0:T(8,128)(2,1)}, u32[]{:S(2)}) copy-start(bf16[1536,512]{1,0:T(8,128)(2,1)} %param.19) | copy-start | bytes 4718596
  7.2 15.6 %copy-start.2 = (bf16[192,1536]{1,0:T(8,128)(2,1)S(1)}, bf16[192,1536]{1,0:T(8,128)(2,1)}, u32[]{:S(2)}) copy-start(bf16[192,1536]{1,0:T(8,128)(2,1)} %param.15) | copy-start | bytes 1769476
  7.2 15.6 %copy-start.11 = (f32[1536]{0:T(1024)S(1)}, f32[1536]{0:T(1024)}, u32[]{:S(2)}) copy-start(f32[1536]{0:T(1024)} %param.17) | copy-start | bytes 18436
  7.2 104.1 %all-gather.4.cloned.1.call-start = ((), (), s32[]{:S(2)}) async-start(), calls=%async_computation.2 | async-start | bytes 6684672 | tf_op jit(solution)/shard_map/all_gather | solution.py:125
  7.2 16.3 %collective-permute-start = (s32[192]{0:T(256)}, s32[192]{0:T(256)S(1)}, u32[]{:S(2)}, u32[]{:S(2)}) collective-permute-start(s32[192]{0:T(256)} %param.16), channel_id=1, source_target_pairs={{0,1},{1,2},{2,3},{3,4},{4,5},{5,6},{6,7},{7,8},{8,9},{9,10},{10,1... | collective-permute-start | bytes 2312 | tf_op jit(solution)/shard_map/ppermute | solution.py:79
  9.3 14.9 %collective-permute-start.9 = (s32[192]{0:T(256)}, s32[192]{0:T(256)S(1)}, u32[]{:S(2)}, u32[]{:S(2)}) collective-permute-start(s32[192]{0:T(256)} %param.16), channel_id=1, source_target_pairs={{0,10},{1,11},{2,12},{3,13},{4,14},{5,15},{6,0},{7,1},{8,2},{9,3},... | collective-permute-start | bytes 2312 | tf_op jit(solution)/shard_map/ppermute | solution.py:79
  15.4 11.3 %collective-permute-start.10 = (s32[192]{0:T(256)}, s32[192]{0:T(256)S(1)}, u32[]{:S(2)}, u32[]{:S(2)}) collective-permute-start(s32[192]{0:T(256)} %param.16), channel_id=1, source_target_pairs={{0,11},{1,12},{2,13},{3,14},{4,15},{5,0},{6,1},{7,2},{8,3},{9,4},{... | collective-permute-start | bytes 2312 | tf_op jit(solution)/shard_map/ppermute | solution.py:79
  16.3 13.1 %collective-permute-start.11 = (s32[192]{0:T(256)}, s32[192]{0:T(256)S(1)}, u32[]{:S(2)}, u32[]{:S(2)}) collective-permute-start(s32[192]{0:T(256)} %param.16), channel_id=1, source_target_pairs={{0,12},{1,13},{2,14},{3,15},{4,0},{5,1},{6,2},{7,3},{8,4},{9,5},{1... | collective-permute-start | bytes 2312 | tf_op jit(solution)/shard_map/ppermute | solution.py:79
  17.5 11.9 %collective-permute-start.12 = (s32[192]{0:T(256)}, s32[192]{0:T(256)S(1)}, u32[]{:S(2)}, u32[]{:S(2)}) collective-permute-start(s32[192]{0:T(256)} %param.16), channel_id=1, source_target_pairs={{0,13},{1,14},{2,15},{3,0},{4,1},{5,2},{6,3},{7,4},{8,5},{9,6},{10... | collective-permute-start | bytes 2312 | tf_op jit(solution)/shard_map/ppermute | solution.py:79
  19.5 3.3 copy-start.10
  20.9 2.5 copy-start.8
  20.9 2.7 copy-start.7
  22.8 26.0 %copy-start.3 = (bf16[36,1536]{1,0:T(8,128)(2,1)S(1)}, bf16[36,1536]{1,0:T(8,128)(2,1)}, u32[]{:S(2)}) copy-start(bf16[36,1536]{1,0:T(8,128)(2,1)} %param.27) | copy-start | bytes 331780
  22.8 25.9 %copy-start.4 = (bf16[36,1536]{1,0:T(8,128)(2,1)S(1)}, bf16[36,1536]{1,0:T(8,128)(2,1)}, u32[]{:S(2)}) copy-start(bf16[36,1536]{1,0:T(8,128)(2,1)} %param.26) | copy-start | bytes 331780
  22.8 25.9 %copy-start.5 = (bf16[36,1536]{1,0:T(8,128)(2,1)S(1)}, bf16[36,1536]{1,0:T(8,128)(2,1)}, u32[]{:S(2)}) copy-start(bf16[36,1536]{1,0:T(8,128)(2,1)} %param.25) | copy-start | bytes 331780
  23.6 6.7 %collective-permute-start.13 = (s32[192]{0:T(256)S(1)}, s32[192]{0:T(256)S(1)}, u32[]{:S(2)}, u32[]{:S(2)}) collective-permute-start(s32[192]{0:T(256)S(1)} %copy-done.7), channel_id=1, source_target_pairs={{0,14},{1,15},{2,0},{3,1},{4,2},{5,3},{6,4},{7,5},{8,6},{9,7},{10,... | collective-permute-start | bytes 2312 | tf_op jit(solution)/shard_map/ppermute | solution.py:79
  24.2 7.8 %collective-permute-start.14 = (s32[192]{0:T(256)S(1)}, s32[192]{0:T(256)S(1)}, u32[]{:S(2)}, u32[]{:S(2)}) collective-permute-start(s32[192]{0:T(256)S(1)} %copy-done.7), channel_id=1, source_target_pairs={{0,15},{1,0},{2,1},{3,2},{4,3},{5,4},{6,5},{7,6},{8,7},{9,8},{10,9... | collective-permute-start | bytes 2312 | tf_op jit(solution)/shard_map/ppermute | solution.py:79
  26.7 8.7 %collective-permute-start.1 = (s32[192]{0:T(256)S(1)}, s32[192]{0:T(256)S(1)}, u32[]{:S(2)}, u32[]{:S(2)}) collective-permute-start(s32[192]{0:T(256)S(1)} %copy-done.7), channel_id=1, source_target_pairs={{0,2},{1,3},{2,4},{3,5},{4,6},{5,7},{6,8},{7,9},{8,10},{9,11},{10,... | collective-permute-start | bytes 2312 | tf_op jit(solution)/shard_map/ppermute | solution.py:79
  29.4 7.8 %collective-permute-start.2 = (s32[192]{0:T(256)S(1)}, s32[192]{0:T(256)S(1)}, u32[]{:S(2)}, u32[]{:S(2)}) collective-permute-start(s32[192]{0:T(256)S(1)} %copy-done.7), channel_id=1, source_target_pairs={{0,3},{1,4},{2,5},{3,6},{4,7},{5,8},{6,9},{7,10},{8,11},{9,12},{10... | collective-permute-start | bytes 2312 | tf_op jit(solution)/shard_map/ppermute | solution.py:79
  29.4 10.5 %collective-permute-start.3 = (s32[192]{0:T(256)S(1)}, s32[192]{0:T(256)S(1)}, u32[]{:S(2)}, u32[]{:S(2)}) collective-permute-start(s32[192]{0:T(256)S(1)} %copy-done.7), channel_id=1, source_target_pairs={{0,4},{1,5},{2,6},{3,7},{4,8},{5,9},{6,10},{7,11},{8,12},{9,13},{1... | collective-permute-start | bytes 2312 | tf_op jit(solution)/shard_map/ppermute | solution.py:79
  30.3 11.5 %collective-permute-start.4 = (s32[192]{0:T(256)S(1)}, s32[192]{0:T(256)S(1)}, u32[]{:S(2)}, u32[]{:S(2)}) collective-permute-start(s32[192]{0:T(256)S(1)} %copy-done.7), channel_id=1, source_target_pairs={{0,5},{1,6},{2,7},{3,8},{4,9},{5,10},{6,11},{7,12},{8,13},{9,14},{... | collective-permute-start | bytes 2312 | tf_op jit(solution)/shard_map/ppermute | solution.py:79
  32.0 9.8 %collective-permute-start.5 = (s32[192]{0:T(256)S(1)}, s32[192]{0:T(256)S(1)}, u32[]{:S(2)}, u32[]{:S(2)}) collective-permute-start(s32[192]{0:T(256)S(1)} %copy-done.7), channel_id=1, source_target_pairs={{0,6},{1,7},{2,8},{3,9},{4,10},{5,11},{6,12},{7,13},{8,14},{9,15},... | collective-permute-start | bytes 2312 | tf_op jit(solution)/shard_map/ppermute | solution.py:79
  35.3 6.5 %collective-permute-start.6 = (s32[192]{0:T(256)S(1)}, s32[192]{0:T(256)S(1)}, u32[]{:S(2)}, u32[]{:S(2)}) collective-permute-start(s32[192]{0:T(256)S(1)} %copy-done.7), channel_id=1, source_target_pairs={{0,7},{1,8},{2,9},{3,10},{4,11},{5,12},{6,13},{7,14},{8,15},{9,0},... | collective-permute-start | bytes 2312 | tf_op jit(solution)/shard_map/ppermute | solution.py:79
  37.2 5.1 %collective-permute-start.7 = (s32[192]{0:T(256)S(1)}, s32[192]{0:T(256)S(1)}, u32[]{:S(2)}, u32[]{:S(2)}) collective-permute-start(s32[192]{0:T(256)S(1)} %copy-done.7), channel_id=1, source_target_pairs={{0,8},{1,9},{2,10},{3,11},{4,12},{5,13},{6,14},{7,15},{8,0},{9,1},... | collective-permute-start | bytes 2312 | tf_op jit(solution)/shard_map/ppermute | solution.py:79
  39.9 5.7 %collective-permute-start.8 = (s32[192]{0:T(256)S(1)}, s32[192]{0:T(256)S(1)}, u32[]{:S(2)}, u32[]{:S(2)}) collective-permute-start(s32[192]{0:T(256)S(1)} %copy-done.7), channel_id=1, source_target_pairs={{0,9},{1,10},{2,11},{3,12},{4,13},{5,14},{6,15},{7,0},{8,1},{9,2},... | collective-permute-start | bytes 2312 | tf_op jit(solution)/shard_map/ppermute | solution.py:79
  48.5 180.6 %all-gather.6.cloned.1.call-start = ((), (), s32[]{:S(2)}) async-start(), calls=%async_computation.4 | async-start | bytes 6266880 | tf_op jit(solution)/shard_map/all_gather | solution.py:126
  49.6 4.6 %copy-start.9 = (f32[64]{0:T(128)S(1)}, f32[64]{0:T(128)}, u32[]{:S(2)}) copy-start(f32[64]{0:T(128)} %param.21) | copy-start | bytes 772
  217.7 3.8 %copy-start.6 = (f32[1536]{0:T(1024)S(1)}, f32[1536]{0:T(1024)}, u32[]{:S(2)}) copy-start(f32[1536]{0:T(1024)} %param.24) | copy-start | bytes 18436
  224.2 59.9 %all-to-all-start = ((bf16[8,192,1536]{2,1,0:T(8,128)(2,1)}), bf16[8,192,1536]{2,1,0:T(8,128)(2,1)}, u32[]{:S(2)}, u32[]{:S(2)}) async-start(bf16[8,192,1536]{2,1,0:T(8,128)(2,1)} %stack.79), calls=%async_computation | async-start | bytes 9437184 | tf_op jit(solution)/shard_map/all_to_all | solution.py:159
  228.8 113.9 %reduce-scatter.2.cloned.1.call-start = ((), (), s32[]{:S(2)}) async-start(), calls=%async_computation.3 | async-start | bytes 5308416 | tf_op jit(solution)/shard_map/reduce_scatter | solution.py:162
  305.5 39.2 %copy-start.1 = (bf16[1536,512]{1,0:T(8,128)(2,1)S(1)}, bf16[1536,512]{1,0:T(8,128)(2,1)}, u32[]{:S(2)}) copy-start(bf16[1536,512]{1,0:T(8,128)(2,1)} %param.19) | copy-start | bytes 4718596
Sparse Core Ops, SparseCore 0:
  48.7 62.6 all-gather.3
  114.1 59.1 all-gather.5
  305.7 36.9 reduce-scatter.1
